TPU v7x, 32 devices: a whole 2x2x4 slice. The times are simulated.
32 devices in a mesh: groups: 2 (over x), ctx: 8 (over z, y), heads: 2 (over core).
Axes of the slice: x: 2, y: 2, z: 4, core: 2. Of those that a mesh axis runs over, the one named last changes fastest.
Arguments:
- ssm_input: bfloat16 [4, 2048, 8192], P('groups', 'ctx', 'heads'), parts along dimension 0, may hold values from -6 to 6
- b_proj: bfloat16 [4, 2048, 512], P('groups', 'ctx', 'heads'), parts along dimension 0, may hold values from -600 to 600
- c_proj: bfloat16 [4, 2048, 512], P('groups', 'ctx', 'heads'), parts along dimension 0, may hold values from -6 to 6
- step_size: float32 [4, 128, 2048], P('groups', 'heads', 'ctx'), parts along dimension 0, may hold values from 0.01 to 0.04
- log_decay: float32 [4, 128, 2048], P('groups', 'heads', 'ctx'), parts along dimension 0, may hold values from -1 to 0
- skip_gain: float32 [128], P('heads'), may hold values from 0.5 to 1.5
- request_of_slot: int32 [16], P(('groups', 'ctx')), parts along dimension 0, may hold values from 0 to 1, as said below
- new_input: bfloat16 [16, 4, 8192], P(('groups', 'ctx'), None, 'heads'), parts along dimension 0, may hold values from -6 to 6
- new_b: bfloat16 [16, 4, 512], P(('groups', 'ctx'), None, 'heads'), parts along dimension 0, may hold values from -0.5 to 0.5
- new_c: bfloat16 [16, 4, 512], P(('groups', 'ctx'), None, 'heads'), parts along dimension 0, may hold values from -6 to 6
- new_step: float32 [16, 4, 128], P(('groups', 'ctx'), None, 'heads'), parts along dimension 0, may hold values from 0.2 to 1
- new_log_decay: float32 [16, 4, 128], P(('groups', 'ctx'), None, 'heads'), parts along dimension 0, may hold values from -0.3 to -0.02
- out_weight: bfloat16 [8192, 8192], P('heads', 'ctx'), may hold values from -0.0625 to 0.0625
Outputs:
- prefill_out: bfloat16 [4, 2048, 8192], P('groups', 'ctx', 'heads'), parts along dimension 0
- decoded: bfloat16 [16, 4, 8192], P('groups', None, 'ctx'), parts along dimension 0
There are 2 independent parts, one for each index of `groups`. A program takes and returns all parts, laid end to end along the dimension named above; an argument that names none is the same for every part. Nothing has to cross between parts.
Inputs may be any that keep to these rules, and one draw needn't show every extreme that they name: `request_of_slot`: every prompt is named by at least one slot.
All inputs are finite; a program needn't handle non-finite values.
Results may differ from a plain program's by a relative error of at most 0.008.
Values may be sent and summed in bfloat16 or wider, within the bound.
No kernel may reach another device: no remote copies, remote signals or barrier semaphores. Data moves between devices by JAX's collectives and lax.ppermute only.
A program may use at most 320 MiB of HBM per device.

v0:
```python
import jax
import jax.numpy as jnp
from jax import lax
from jax.sharding import PartitionSpec as P

HEADS = 128
HEAD_DIM = 64
STATE = 128
GROUPS = 4
HIGH = lax.Precision.HIGHEST


def block_terms(block_input, block_b, block_c, block_step, block_logd):
    block_size = block_input.shape[0]
    head_count = block_step.shape[0]
    per_group = HEADS // GROUPS
    group_count = head_count // per_group
    cumulative = jnp.cumsum(block_logd, axis=1)
    block_total = cumulative[:, -1]
    inputs_head = block_input.reshape(block_size, group_count, per_group, HEAD_DIM)
    b_groups = block_b.reshape(block_size, group_count, STATE)
    c_groups = block_c.reshape(block_size, group_count, STATE)
    scores = jnp.einsum("tgn,sgn->gts", c_groups, b_groups, preferred_element_type=jnp.float32)
    row_index = lax.broadcasted_iota(jnp.int32, (block_size, block_size), 0)
    col_index = lax.broadcasted_iota(jnp.int32, (block_size, block_size), 1)
    causal = row_index >= col_index
    log_gap = cumulative[:, :, None] - cumulative[:, None, :]
    decay_rate = (
        jnp.where(causal, jnp.exp(jnp.where(causal, log_gap, 0.0)), 0.0) * block_step[:, None, :]
    )
    mixing = (
        scores[:, None, :, :] * decay_rate.reshape(group_count, per_group, block_size, block_size)
    ).astype(jnp.bfloat16)
    local_out = jnp.einsum(
        "gkts,sgkp->tgkp", mixing, inputs_head, preferred_element_type=jnp.float32
    )
    weighting = jnp.exp(block_total[:, None] - cumulative) * block_step
    weighted = (weighting.T.reshape(block_size, group_count, per_group, 1) * inputs_head).astype(
        jnp.bfloat16
    )
    block_state = jnp.einsum(
        "sgkp,sgn->gkpn", weighted, b_groups, preferred_element_type=jnp.float32
    )
    return (cumulative, block_total.reshape(group_count, per_group), local_out, block_state)


def finish(local_out, cumulative, block_c, entering, block_input, skip_gain):
    block_size = block_input.shape[0]
    group_count, per_group = (entering.shape[0], entering.shape[1])
    c_groups = block_c.reshape(block_size, group_count, STATE).astype(jnp.float32)
    carried = jnp.einsum("tgn,gkpn->tgkp", c_groups, entering, precision=HIGH)
    carried = carried * jnp.exp(cumulative).T.reshape(block_size, group_count, per_group, 1)
    inputs_head = block_input.reshape(block_size, group_count, per_group, HEAD_DIM)
    skipped = skip_gain.reshape(group_count, per_group, 1) * inputs_head
    return (
        (local_out + carried + skipped)
        .reshape(block_size, group_count * per_group * HEAD_DIM)
        .astype(jnp.bfloat16)
    )


def range_decay(all_totals, low, high):
    place = lax.broadcasted_iota(jnp.int32, all_totals.shape, 0)
    keep = (place >= low) & (place <= high)
    return jnp.exp(jnp.sum(jnp.where(keep, all_totals, 0.0), axis=0))


def scale(factor, state):
    return factor[..., None, None] * state


def send(value, pairs):
    return lax.ppermute(value.astype(jnp.bfloat16), "ctx", pairs).astype(jnp.float32)


def prefix_states(states, all_totals):
    count = lax.axis_size("ctx")
    columns = count // 2
    place = lax.axis_index("ctx")
    row = place % 2
    column = place // 2
    half = states.shape[-2] // 2
    first = states[..., :half, :]
    second = states[..., half:, :]
    row_zero = row == 0
    mine = jnp.where(row_zero, first, second)
    other = jnp.where(row_zero, second, first)
    across = [(2 * m, 2 * m + 1) for m in range(columns)] + [
        (2 * m + 1, 2 * m) for m in range(columns)
    ]
    received = send(other, across)
    even_state = jnp.where(row_zero, mine, received)
    odd_state = jnp.where(row_zero, received, mine)
    odd_decay = range_decay(all_totals, 2 * column + 1, 2 * column + 1)
    window = scale(odd_decay, even_state) + odd_state
    before = jnp.zeros_like(window)
    step = 1
    while step < columns:
        pairs = [(y + 2 * m, y + 2 * (m + step)) for y in range(2) for m in range(columns - step)]
        got = send(window, pairs)
        low = 2 * (column - step) + 2
        before = scale(range_decay(all_totals, low, 2 * column - 1), got) + before
        if 2 * step < columns:
            window = scale(range_decay(all_totals, low, 2 * column + 1), got) + window
        step *= 2
    even_decay = range_decay(all_totals, 2 * column, 2 * column)
    odd_entering = scale(even_decay, before) + even_state
    outgoing = jnp.where(row_zero, odd_entering, before)
    partner = send(outgoing, across)
    own_half = jnp.where(row_zero, before, odd_entering)
    first_half = jnp.where(row_zero, own_half, partner)
    second_half = jnp.where(row_zero, partner, own_half)
    return jnp.concatenate([first_half, second_half], axis=-2)


def shards(
    ssm_input,
    b_proj,
    c_proj,
    step_size,
    log_decay,
    skip_gain,
    request_of_slot,
    new_input,
    new_b,
    new_c,
    new_step,
    new_log_decay,
    out_weight,
):
    request_count = ssm_input.shape[0]
    count = lax.axis_size("ctx")
    place = lax.axis_index("ctx")
    terms = []
    for request in range(request_count):
        terms.append(
            block_terms(
                ssm_input[request],
                b_proj[request],
                c_proj[request],
                step_size[request],
                log_decay[request],
            )
        )
    totals = jnp.stack([term[1] for term in terms])
    states = jnp.stack([term[3] for term in terms])
    group_count, per_group = (totals.shape[1], totals.shape[2])
    slots, steps = (new_input.shape[0], new_input.shape[1])
    pieces = [
        totals,
        request_of_slot.astype(jnp.float32),
        new_input.astype(jnp.float32),
        new_b.astype(jnp.float32),
        new_c.astype(jnp.float32),
        new_step,
        new_log_decay,
    ]
    packed = jnp.concatenate([piece.reshape(-1) for piece in pieces])
    gathered = lax.all_gather(packed, "ctx")
    unpacked = []
    offset = 0
    for piece in pieces:
        size = piece.size
        unpacked.append(gathered[:, offset : offset + size].reshape((count,) + piece.shape))
        offset += size
    all_totals, all_request, all_input, all_b, all_c, all_step, all_logd = unpacked
    all_slots = count * slots
    all_request = all_request.reshape(all_slots)
    all_input = all_input.reshape(all_slots, steps, group_count, per_group, HEAD_DIM)
    all_b = all_b.reshape(all_slots, steps, group_count, STATE)
    all_c = all_c.reshape(all_slots, steps, group_count, STATE)
    all_step = all_step.reshape(all_slots, steps, group_count, per_group)
    all_logd = all_logd.reshape(all_slots, steps, group_count, per_group)
    later = range_decay(all_totals, place + 1, count - 1)
    weighted_states = scale(later, states)
    projected = jnp.einsum("rgkpn,jugn->rjugkp", weighted_states, all_c, precision=HIGH)
    request_numbers = lax.broadcasted_iota(jnp.int32, (request_count, 1), 0).astype(jnp.float32)
    chosen = (request_numbers == all_request[None, :]).astype(jnp.float32)
    contribution = jnp.einsum("rj,rjugkp->jugkp", chosen, projected, precision=HIGH)
    from_prompt = lax.psum(contribution, "ctx")
    cum_logd = jnp.cumsum(all_logd, axis=1)
    inner = jnp.einsum("jvgn,jugn->jvug", all_b, all_c, precision=HIGH)
    driven = all_step[..., None] * all_input
    outputs = []
    for u in range(steps):
        value = jnp.exp(cum_logd[:, u])[..., None] * from_prompt[:, u]
        for v in range(u + 1):
            gap = jnp.exp(cum_logd[:, u] - cum_logd[:, v])
            coefficient = gap * inner[:, v, u][:, :, None]
            value = value + coefficient[..., None] * driven[:, v]
        value = value + skip_gain.reshape(group_count, per_group, 1) * all_input[:, u]
        outputs.append(value.reshape(all_slots, -1).astype(jnp.bfloat16))
    new_output = jnp.stack(outputs, axis=1)
    partial_value = jnp.einsum(
        "jup,pd->jud", new_output, out_weight, preferred_element_type=jnp.float32
    )
    decoded = lax.psum(partial_value, "heads").astype(jnp.bfloat16)
    entering = prefix_states(states, all_totals)
    prefill_rows = []
    for request in range(request_count):
        prefill_rows.append(
            finish(
                terms[request][2],
                terms[request][0],
                c_proj[request],
                entering[request],
                ssm_input[request],
                skip_gain,
            )
        )
    prefill_out = jnp.stack(prefill_rows)
    return (prefill_out, decoded)


def solution(mesh):
    in_specs = (
        P("groups", "ctx", "heads"),
        P("groups", "ctx", "heads"),
        P("groups", "ctx", "heads"),
        P("groups", "heads", "ctx"),
        P("groups", "heads", "ctx"),
        P("heads"),
        P(("groups", "ctx")),
        P(("groups", "ctx"), None, "heads"),
        P(("groups", "ctx"), None, "heads"),
        P(("groups", "ctx"), None, "heads"),
        P(("groups", "ctx"), None, "heads"),
        P(("groups", "ctx"), None, "heads"),
        P("heads", "ctx"),
    )
    out_specs = (P("groups", "ctx", "heads"), P("groups", None, "ctx"))
    return jax.shard_map(shards, mesh=mesh, in_specs=in_specs, out_specs=out_specs, check_vma=False)
```

profile of v0, /device:TPU:26, one launch (start us, length us, event | category | flops | bytes accessed | tf_op | source)
XLA Modules:
  0.0 315.2 jit_solution(35564834466314363)
XLA Ops:
  19.5 3.9 %fusion.76 = (bf16[1,256,4096]{2,1,0:T(8,128)(2,1)}, bf16[1,256,4096]{2,1,0:T(8,128)(2,1)S(1)}) fusion(bf16[2,256,4096]{2,1,0:T(8,128)(2,1)} %param.13), kind=kLoop, calls=%fused_computation.144 | loop fusion | bytes 8388608 | tf_op jit(solution)/shard_map/slice | solution.py:138
  23.4 4.2 %copy.105 = bf16[1,256,4096]{1,2,0:T(8,128)(2,1)} copy(bf16[1,256,4096]{2,1,0:T(8,128)(2,1)} %get-tuple-element.18) | data formatting | bytes 4194304 | tf_op jit(solution)/shard_map/slice | solution.py:138
  27.7 2.5 copy.110
  30.4 2.5 fusion.52
  45.4 8.0 %fusion = f32[2,32,256,64]{2,3,1,0:T(8,128)} fusion(bf16[256,2,32,64]{0,3,2,1:T(8,128)(2,1)} %bitcast.245, f32[2,32,256]{2,1,0:T(8,128)} %bitcast.270, f32[2,32,256]{2,1,0:T(8,128)} %reduce_window_sum.59, f32[2,256,256]{2,1,0:T(8,128)S(1)} %fusion.88, pred[256,256]{1,0:T(8,128)(4,1)} %iota_compare_fusion), kind=kOutput, calls=%fused_computation.2 | convolution fusion | flops 562036736 | bytes 7012352 | tf_op jit(solution)/shard_map/gkts,sgkp->tgkp/dot_general | solution.py:34
  53.4 6.6 %fusion.1 = f32[2,32,256,64]{2,3,1,0:T(8,128)} fusion(bf16[256,2,32,64]{0,3,2,1:T(8,128)(2,1)S(1)} %bitcast.248, f32[2,32,256]{2,1,0:T(8,128)S(1)} %bitcast.269, f32[2,32,256]{2,1,0:T(8,128)S(1)} %copy-done.32, f32[2,256,256]{2,1,0:T(8,128)S(1)} %fusion.89, pred[256,256]{1,0:T(8,128)(4,1)S(1)} %copy-done.31), kind=kOutput, calls=%fused_computation.3 | convolution fusion | flops 562036736 | bytes 7012352 | tf_op jit(solution)/shard_map/gkts,sgkp->tgkp/dot_general | solution.py:34
  62.5 30.0 %all-reduce.7.cloned.1.call-done = f32[152584]{0:T(1024)} async-done(((f32[152584]{0:T(1024)}), f32[152584]{0:T(1024)}) %all-reduce.7.cloned.1.call-update) | async-done | bytes 610352
  113.2 12.9 %fusion.49 = f32[2,8,4,2,32,64]{5,1,4,0,2,3:T(8,128)S(1)} fusion(f32[8,4,2,128,1,1]{3,0,2,1,5,4:T(8,128)S(1)} %bitcast.262, f32[1,2,32,64,128]{4,3,2,1,0:T(8,128)} %copy-done, f32[1,2,32,64,128]{4,3,2,1,0:T(8,128)S(1)} %fusion.52, f32[2,2,32]{2,1,0:T(2,128)S(1)} %exp.239), kind=kOutput, calls=%fused_computation.71 | convolution fusion | flops 404750336 | bytes 5276160 | tf_op jit(solution)/shard_map/rgkpn,jugn->rjugkp/dot_general | solution.py:176
  126.1 4.9 %fusion.47 = f32[8,1,4,2,32,64]{5,1,4,3,2,0:T(1,128)S(1)} fusion(pred[2,8,1,1,1,1]{0,2,5,4,3,1:T(4,128)(4,1)S(1)} %copy.162, f32[2,8,4,2,32,64]{5,1,4,0,2,3:T(8,128)S(1)} %fusion.49), kind=kOutput, calls=%fused_computation.69 | convolution fusion | flops 3145728 | bytes 1572880 | tf_op jit(solution)/shard_map/rj,rjugkp->jugkp/dot_general | solution.py:179
  132.1 2.5 reshape_reshape.15
  134.7 3.9 %fusion.58 = (bf16[2,2,32,32,128]{4,3,2,1,0:T(8,128)(2,1)}, f32[2,2,32,32,128]{4,3,2,1,0:T(8,128)}) fusion(bf16[2,2,32,32,128]{4,3,2,1,0:T(8,128)(2,1)S(1)} %collective-permute-done, pred[]{:T(512)S(6)} %eq.20, f32[2,2,32]{2,1,0:T(2,128)S(1)} %exp.226, f32[1,2,32,64,128]{4,3,2,1,0:T(8,128)} %copy-done, f32[1,2,32,64,128]{4,3,2,1,0:T(8,128)S(1)} %fusion.52), kind=kLoop, calls=%fused_computation.77 | loop fusion | flops 4718592 | bytes 8389121 | tf_op jit(solution)/shard_map/convert_element_type | solution.py:73
  185.1 3.0 fusion.30
  189.4 53.2 %all-reduce.5.cloned.1.call-done = f32[8,4,2,32,64]{4,3,2,0,1:T(8,128)} async-done(((f32[8,4,2,32,64]{4,3,2,0,1:T(8,128)}), f32[8,4,2,32,64]{4,3,2,0,1:T(8,128)}) %all-reduce.5.cloned.1.call-update) | async-done | bytes 524304 | tf_op jit(solution)/shard_map/psum | solution.py:180
  253.6 3.1 select_convert_fusion
  256.6 7.5 %collective-permute-start.3 = (bf16[2,2,32,32,128]{4,3,2,1,0:T(8,128)(2,1)}, bf16[2,2,32,32,128]{4,3,2,1,0:T(8,128)(2,1)}, u32[]{:S(2)}, u32[]{:S(2)}) collective-permute-start(bf16[2,2,32,32,128]{4,3,2,1,0:T(8,128)(2,1)} %select_convert_fusion), channel_id=1, source_target_pairs={{0,2},{4,6},{8,10},{12,14},{2,0},{6,4},{10,8},{14,12},{1,3},{5,7},... | collective-permute-start | bytes 3145736 | tf_op jit(solution)/shard_map/ppermute | solution.py:73
  264.4 4.9 %fusion.2 = f32[8,4,1024]{2,0,1:T(8,128)S(1)} fusion(bf16[4096,1024]{1,0:T(8,128)(2,1)} %param.25, bf16[8,1,4096]{2,0,1:T(8,128)(2,1)S(1)} %get-tuple-element.37, bf16[8,1,4096]{2,0,1:T(8,128)(2,1)S(1)} %get-tuple-element.36, bf16[8,1,4096]{2,0,1:T(8,128)(2,1)S(1)} %get-tuple-element.43, bf16[8,1,4096]{2,0,1:T(8,128)(2,1)S(1)} %get-tuple-element.42), kind=kOutput, calls=%fused_computation.4 | convolution fusion | flops 268828672 | bytes 8781824 | tf_op jit(solution)/shard_map/jup,pd->jud/dot_general | solution.py:194
  269.2 4.4 %all-reduce.8 = bf16[8,4,1024]{2,0,1:T(8,128)(2,1)} all-reduce(f32[8,4,1024]{2,0,1:T(8,128)S(1)} %fusion.2), channel_id=1, replica_groups=mesh['groups'=2,'ctx'=8,'heads'=2] {'heads'}, use_global_device_ids=true, to_apply=%region_12.13 | all-reduce | flops 32768 | bytes 196608 | tf_op jit(solution)/shard_map/psum | solution.py:197
  275.1 6.9 %collective-permute-done.3 = bf16[2,2,32,32,128]{4,3,2,1,0:T(8,128)(2,1)} collective-permute-done((bf16[2,2,32,32,128]{4,3,2,1,0:T(8,128)(2,1)}, bf16[2,2,32,32,128]{4,3,2,1,0:T(8,128)(2,1)}, u32[]{:S(2)}, u32[]{:S(2)}) %collective-permute-start.3) | collective-permute-done | bytes 1048608 | tf_op jit(solution)/shard_map/ppermute | solution.py:73
  282.0 2.8 convert_select_fusion.1
  285.2 4.0 %fusion.18 = bf16[256,2,32,64]{0,3,2,1:T(8,128)(2,1)} fusion(bf16[256,2,32,64]{0,3,2,1:T(8,128)(2,1)S(1)} %bitcast.246, f32[2,32,256,64]{2,3,1,0:T(8,128)S(1)} %copy-done.11, bf16[256,2,128,1]{0,2,3,1:T(8,128)(2,1)S(1)} %bitcast.256, f32[2,2,32,32,128]{4,3,2,1,0:T(8,128)S(1)} %get-tuple-element.16, f32[2,2,32,32,128]{4,3,2,1,0:T(8,128)S(1)} %get-tuple-element.17, ...), kind=kOutput, calls=%fused_computation.29 | convolution fusion | flops 1617428480 | bytes 12779776 | tf_op jit(solution)/shard_map/tgn,gkpn->tgkp/dot_general | solution.py:51
  289.2 4.4 %copy.119 = bf16[1,256,4096]{2,1,0:T(8,128)(2,1)} copy(bf16[1,256,4096]{1,2,0:T(8,128)(2,1)} %bitcast.251) | data formatting | bytes 4194304 | tf_op jit(solution)/shard_map/convert_element_type | solution.py:58
  293.5 6.6 %fusion.21 = bf16[256,2,32,64]{0,3,2,1:T(8,128)(2,1)} fusion(bf16[256,2,32,64]{0,3,2,1:T(8,128)(2,1)S(1)} %bitcast.249, f32[2,32,256,64]{2,3,1,0:T(8,128)} %fusion.1, bf16[256,2,128,1]{0,2,3,1:T(8,128)(2,1)S(1)} %bitcast.254, f32[2,2,32,32,128]{4,3,2,1,0:T(8,128)} %copy-done.7, f32[2,2,32,32,128]{4,3,2,1,0:T(8,128)} %copy-done.6, ...), kind=kOutput, calls=%fused_computation.32 | convolution fusion | flops 1617428480 | bytes 12779776 | tf_op jit(solution)/shard_map/tgn,gkpn->tgkp/dot_general | solution.py:51
  300.1 4.3 %copy.120 = bf16[1,256,4096]{2,1,0:T(8,128)(2,1)} copy(bf16[1,256,4096]{1,2,0:T(8,128)(2,1)} %bitcast.250) | data formatting | bytes 4194304 | tf_op jit(solution)/shard_map/convert_element_type | solution.py:58
  304.4 4.0 %pad_maximum_fusion.1 = bf16[2,256,4096]{2,1,0:T(8,128)(2,1)} fusion(bf16[1,256,4096]{2,1,0:T(8,128)(2,1)} %copy.120, bf16[1,256,4096]{2,1,0:T(8,128)(2,1)S(1)} %copy-done.10), kind=kLoop, calls=%fused_computation.37 | loop fusion | flops 2097152 | bytes 8388608 | tf_op jit(solution)/shard_map/stack | solution.py:211
  (270 shorter events, 108.3 us)
Async XLA Ops:
  7.2 11.5 %copy-start.24 = (f32[2,64,256]{2,1,0:T(8,128)S(1)}, f32[2,64,256]{2,1,0:T(8,128)}, u32[]{:S(2)}) copy-start(f32[2,64,256]{2,1,0:T(8,128)} %param.16) | copy-start | bytes 393220
  7.2 85.3 %all-reduce.7.cloned.1.call-start = ((), (), s32[]{:S(2)}) async-start(), calls=%async_computation.1 | async-start | bytes 1228800
  18.6 224.0 %all-reduce.5.cloned.1.call-start = ((), (), s32[]{:S(2)}) async-start(), calls=%async_computation | async-start | bytes 2097152 | tf_op jit(solution)/shard_map/psum | solution.py:180
  35.3 99.4 %collective-permute-start = (bf16[2,2,32,32,128]{4,3,2,1,0:T(8,128)(2,1)}, bf16[2,2,32,32,128]{4,3,2,1,0:T(8,128)(2,1)S(1)}, u32[]{:S(2)}, u32[]{:S(2)}) collective-permute-start(bf16[2,2,32,32,128]{4,3,2,1,0:T(8,128)(2,1)} %select_convert_fusion.1), channel_id=1, source_target_pairs={{0,2},{4,6},{8,10},{12,14},{2,0},{6,4},{10,8},{14,12},{1,3},{5,7},... | collective-permute-start | bytes 3145736 | tf_op jit(solution)/shard_map/ppermute | solution.py:73
  60.1 32.4 %copy-start.48 = (f32[2,32]{1,0:T(2,128)}, f32[2,32]{1,0:T(2,128)S(1)}, u32[]{:S(2)}) copy-start(f32[2,32]{1,0:T(2,128)S(1)} %mul.656) | copy-start | bytes 772
  138.6 46.6 %collective-permute-start.1 = (bf16[2,2,32,32,128]{4,3,2,1,0:T(8,128)(2,1)}, bf16[2,2,32,32,128]{4,3,2,1,0:T(8,128)(2,1)}, u32[]{:S(2)}, u32[]{:S(2)}) collective-permute-start(bf16[2,2,32,32,128]{4,3,2,1,0:T(8,128)(2,1)} %get-tuple-element.14), channel_id=1, source_target_pairs={{0,4},{4,8},{8,12},{2,6},{6,10},{10,14},{1,5},{5,9},{9,13},{3,7},{... | collective-permute-start | bytes 3145736 | tf_op jit(solution)/shard_map/ppermute | solution.py:73
  156.7 28.4 %copy-start.1 = (f32[2,2,32,32,128]{4,3,2,1,0:T(8,128)S(1)}, f32[2,2,32,32,128]{4,3,2,1,0:T(8,128)}, u32[]{:S(2)}) copy-start(f32[2,2,32,32,128]{4,3,2,1,0:T(8,128)} %get-tuple-element.15) | copy-start | bytes 6291460
  188.1 65.4 %collective-permute-start.2 = (bf16[2,2,32,32,128]{4,3,2,1,0:T(8,128)(2,1)}, bf16[2,2,32,32,128]{4,3,2,1,0:T(8,128)(2,1)}, u32[]{:S(2)}, u32[]{:S(2)}) collective-permute-start(bf16[2,2,32,32,128]{4,3,2,1,0:T(8,128)(2,1)} %fusion.30), channel_id=1, source_target_pairs={{0,8},{4,12},{2,10},{6,14},{1,9},{5,13},{3,11},{7,15},{16,24},{20,... | collective-permute-start | bytes 3145736 | tf_op jit(solution)/shard_map/ppermute | solution.py:73
  253.4 10.7 %copy-start.13 = (f32[8,1,4096]{2,0,1:T(8,128)S(1)}, f32[8,1,4096]{2,0,1:T(8,128)}, u32[]{:S(2)}) copy-start(f32[8,1,4096]{2,0,1:T(8,128)} %squeeze.40) | copy-start | bytes 393220
  253.4 10.7 %copy-start.15 = (f32[8,1,4096]{2,0,1:T(8,128)S(1)}, f32[8,1,4096]{2,0,1:T(8,128)}, u32[]{:S(2)}) copy-start(f32[8,1,4096]{2,0,1:T(8,128)} %mul.677) | copy-start | bytes 393220
  253.5 10.7 %copy-start.16 = (f32[8,1,4096]{2,0,1:T(8,128)S(1)}, f32[8,1,4096]{2,0,1:T(8,128)}, u32[]{:S(2)}) copy-start(f32[8,1,4096]{2,0,1:T(8,128)} %mul.693) | copy-start | bytes 393220
  253.5 10.7 %copy-start.17 = (f32[8,1,4096]{2,0,1:T(8,128)S(1)}, f32[8,1,4096]{2,0,1:T(8,128)}, u32[]{:S(2)}) copy-start(f32[8,1,4096]{2,0,1:T(8,128)} %mul.699) | copy-start | bytes 393220
  253.5 10.7 %copy-start.18 = (f32[8,1,4096]{2,0,1:T(8,128)S(1)}, f32[8,1,4096]{2,0,1:T(8,128)}, u32[]{:S(2)}) copy-start(f32[8,1,4096]{2,0,1:T(8,128)} %mul.669) | copy-start | bytes 393220
  253.5 10.7 %copy-start.19 = (f32[8,1,4096]{2,0,1:T(8,128)S(1)}, f32[8,1,4096]{2,0,1:T(8,128)}, u32[]{:S(2)}) copy-start(f32[8,1,4096]{2,0,1:T(8,128)} %mul.687) | copy-start | bytes 393220
  253.5 10.7 %copy-start.20 = (f32[8,1,4096]{2,0,1:T(8,128)S(1)}, f32[8,1,4096]{2,0,1:T(8,128)}, u32[]{:S(2)}) copy-start(f32[8,1,4096]{2,0,1:T(8,128)} %squeeze.38) | copy-start | bytes 393220
  253.5 10.7 %copy-start.21 = (f32[8,1,4096]{2,0,1:T(8,128)S(1)}, f32[8,1,4096]{2,0,1:T(8,128)}, u32[]{:S(2)}) copy-start(f32[8,1,4096]{2,0,1:T(8,128)} %squeeze.41) | copy-start | bytes 393220
  253.5 10.7 %copy-start.22 = (f32[8,1,4096]{2,0,1:T(8,128)S(1)}, f32[8,1,4096]{2,0,1:T(8,128)}, u32[]{:S(2)}) copy-start(f32[8,1,4096]{2,0,1:T(8,128)} %squeeze.36) | copy-start | bytes 393220
  253.5 10.7 %copy-start.23 = (f32[8,1,4096]{2,0,1:T(8,128)S(1)}, f32[8,1,4096]{2,0,1:T(8,128)}, u32[]{:S(2)}) copy-start(f32[8,1,4096]{2,0,1:T(8,128)} %squeeze.39) | copy-start | bytes 393220
  256.6 25.4 %collective-permute-start.3 = (bf16[2,2,32,32,128]{4,3,2,1,0:T(8,128)(2,1)}, bf16[2,2,32,32,128]{4,3,2,1,0:T(8,128)(2,1)}, u32[]{:S(2)}, u32[]{:S(2)}) collective-permute-start(bf16[2,2,32,32,128]{4,3,2,1,0:T(8,128)(2,1)} %select_convert_fusion), channel_id=1, source_target_pairs={{0,2},{4,6},{8,10},{12,14},{2,0},{6,4},{10,8},{14,12},{1,3},{5,7},... | collective-permute-start | bytes 3145736 | tf_op jit(solution)/shard_map/ppermute | solution.py:73
  264.3 17.7 %copy-start.43 = (f32[2,2,32]{2,1,0:T(2,128)S(1)}, f32[2,2,32]{2,1,0:T(2,128)}, u32[]{:S(2)}) copy-start(f32[2,2,32]{2,1,0:T(2,128)} %exp.222) | copy-start | bytes 1540
  264.4 17.7 %copy-start.45 = (f32[2,2,32]{2,1,0:T(2,128)S(1)}, f32[2,2,32]{2,1,0:T(2,128)}, u32[]{:S(2)}) copy-start(f32[2,2,32]{2,1,0:T(2,128)} %exp.230) | copy-start | bytes 1540
  264.4 17.7 %copy-start.47 = (f32[2,2,32]{2,1,0:T(2,128)S(1)}, f32[2,2,32]{2,1,0:T(2,128)}, u32[]{:S(2)}) copy-start(f32[2,2,32]{2,1,0:T(2,128)} %exp.232) | copy-start | bytes 1540
  275.1 9.8 %copy-start.29 = (f32[64,256]{1,0:T(8,128)S(1)}, f32[64,256]{1,0:T(8,128)}, u32[]{:S(2)}) copy-start(f32[64,256]{1,0:T(8,128)} %get-tuple-element.51) | copy-start | bytes 196612
  275.1 9.8 %copy-start.49 = (f32[2,32]{1,0:T(2,128)S(1)}, f32[2,32]{1,0:T(2,128)}, u32[]{:S(2)}) copy-start(f32[2,32]{1,0:T(2,128)} %copy-done.48) | copy-start | bytes 772
  (33 other events, 146.7 us)
Sparse Core Ops, SparseCore 0:
  18.8 73.6 all-reduce.6
  132.2 110.3 all-reduce.4
where the time goes:
time: 317 us; the launch traced here: 315 us
  local copies, waits for them, and re-layouts  109 us (34%)
  waiting for transfers between devices  90.2 us (28%)
  matrix products  52.7 us (17%)
  other arithmetic  31.6 us (10%)
  between operations  16.2 us (5%)
  starting transfers between devices  11.6 us (4%)
  blocking collectives  4.36 us (1%)
    psum x1, waiting for transfers between devices, shards(): from_prompt = lax.psum(contribution, 'ctx')  53.2 us
    unnamed x3, waiting for transfers between devices  30 us
    mul x20, local copies, waits for them, and re-layouts, shards(): value = value + coefficient[..., None] * driven[:, v]  15.8 us
    dot_general x2, matrix products, block_terms(): jnp.einsum('gkts,sgkp->tgkp', mixing, inputs_head, preferred_element_type...  14.6 us
    dot_general x1, matrix products, shards(): jnp.einsum('rgkpn,jugn->rjugkp', weighted_states, all_c, precision=HIGH)  12.9 us
    convert_element_type x4, other arithmetic, send(): value.astype(jnp.bfloat16)  11.5 us
    ppermute x4, starting transfers between devices, send(): lax.ppermute(value.astype(jnp.bfloat16), 'ctx', pairs).astype(jnp.float32)  11.5 us
    slice x3, local copies, waits for them, and re-layouts, shards(): ssm_input[request]  10.6 us
  transfers between devices with their start and end apart: 6, of which 3 were waited for; matrix products, arithmetic and copies ran while one was open for 48% of the time, Pallas kernels for 0%

commit v1 on v0

--- a/solution.py
+++ b/solution.py
@@ -177,7 +177,7 @@
     request_numbers = lax.broadcasted_iota(jnp.int32, (request_count, 1), 0).astype(jnp.float32)
     chosen = (request_numbers == all_request[None, :]).astype(jnp.float32)
     contribution = jnp.einsum("rj,rjugkp->jugkp", chosen, projected, precision=HIGH)
-    from_prompt = lax.psum(contribution, "ctx")
+    from_prompt = jnp.sum(lax.all_gather(contribution, "ctx"), axis=0)
     cum_logd = jnp.cumsum(all_logd, axis=1)
     inner = jnp.einsum("jvgn,jugn->jvug", all_b, all_c, precision=HIGH)
     driven = all_step[..., None] * all_input

time: 317 us -> 411 us (1.30)
  waiting for transfers between devices: 90.2 us -> 176 us
  local copies, waits for them, and re-layouts: 109 us -> 116 us
  starting transfers between devices: 11.6 us -> 5.57 us
    ppermute x4, waiting for transfers between devices: 6.9 us -> 128 us  [send(): lax.ppermute(value.astype(jnp.bfloat16), 'ctx', pairs).astype(jnp.float32)]
    psum x1 -> x0, waiting for transfers between devices: 53.2 us -> none  [shards(): from_prompt = lax.psum(contribution, 'ctx')]
    unnamed x3, waiting for transfers between devices: 30 us -> 48.1 us
    mul x20, local copies, waits for them, and re-layouts: 15.8 us -> 25.5 us  [shards(): value = value + coefficient[..., None] * driven[:, v]]
    ppermute x4, starting transfers between devices: 11.5 us -> 5.49 us  [send(): lax.ppermute(value.astype(jnp.bfloat16), 'ctx', pairs).astype(jnp.float32)]
    exp x12, local copies, waits for them, and re-layouts: 9.99 us -> 4.22 us  [range_decay(): return jnp.exp(jnp.sum(jnp.where(keep, all_totals, 0.0), axis=0))]
    squeeze x4, local copies, waits for them, and re-layouts: 6.87 us -> 1.78 us  [shards(): value = jnp.exp(cum_logd[:, u])[..., None] * from_prompt[:, u]]
    reduce_sum x0 -> x1, other arithmetic: none -> 4.58 us  [shards(): from_prompt = jnp.sum(lax.all_gather(contribution, 'ctx'), axis=0)]
  transfers between devices with their start and end apart: 6 -> 6, of which waited for: 3 -> 3; matrix products, arithmetic and copies ran while one was open for 48% -> 44% of each run, Pallas kernels for 0% -> 0%
where the time goes in v1:
time: 411 us; the launch traced here: 408 us
  waiting for transfers between devices  176 us (43%)
  local copies, waits for them, and re-layouts  116 us (28%)
  matrix products  54.9 us (13%)
  other arithmetic  35.5 us (9%)
  between operations  16.4 us (4%)
  starting transfers between devices  5.57 us (1%)
    ppermute x4, waiting for transfers between devices, send(): lax.ppermute(value.astype(jnp.bfloat16), 'ctx', pairs).astype(jnp.float32)  128 us
    unnamed x3, waiting for transfers between devices  48.1 us
    mul x20, local copies, waits for them, and re-layouts, shards(): value = value + coefficient[..., None] * driven[:, v]  25.5 us
    dot_general x2, matrix products, block_terms(): jnp.einsum('gkts,sgkp->tgkp', mixing, inputs_head, preferred_element_type...  14.4 us
    unnamed x141, local copies, waits for them, and re-layouts  13.8 us
    dot_general x1, matrix products, shards(): jnp.einsum('rgkpn,jugn->rjugkp', weighted_states, all_c, precision=HIGH)  12.9 us
    convert_element_type x4, other arithmetic, send(): value.astype(jnp.bfloat16)  11.4 us
    dot_general x2, matrix products, finish(): carried = jnp.einsum('tgn,gkpn->tgkp', c_groups, entering, precision=HIGH)  10.6 us
  transfers between devices with their start and end apart: 6, of which 3 were waited for; matrix products, arithmetic and copies ran while one was open for 44% of the time, Pallas kernels for 0%

profile of v1, /device:TPU:26, one launch (start us, length us, event | category | flops | bytes accessed | tf_op | source)
XLA Modules:
  0.0 408.5 jit_solution(5696635481940201439)
XLA Ops:
  19.5 3.9 fusion.76
  23.4 4.1 %copy.211 = bf16[1,256,4096]{1,2,0:T(8,128)(2,1)} copy(bf16[1,256,4096]{2,1,0:T(8,128)(2,1)} %get-tuple-element.22) | data formatting | bytes 4194304 | tf_op jit(solution)/shard_map/slice | solution.py:138
  27.7 2.5 copy.216
  44.5 48.0 %all-reduce.4.cloned.1.call-done = f32[152584]{0:T(1024)} async-done(((f32[152584]{0:T(1024)}), f32[152584]{0:T(1024)}) %all-reduce.4.cloned.1.call-update) | async-done | bytes 610352
  98.8 12.9 %fusion.49 = f32[2,8,4,2,32,64]{5,1,4,0,2,3:T(8,128)S(1)} fusion(f32[8,4,2,128,1,1]{3,0,2,1,5,4:T(8,128)S(1)} %bitcast.254, f32[1,2,32,64,128]{4,3,2,1,0:T(8,128)} %copy-done, f32[1,2,32,64,128]{4,3,2,1,0:T(8,128)S(1)} %fusion.52, f32[2,2,32]{2,1,0:T(2,128)S(1)} %exp.239), kind=kOutput, calls=%fused_computation.71 | convolution fusion | flops 404750336 | bytes 5276160 | tf_op jit(solution)/shard_map/rgkpn,jugn->rjugkp/dot_general | solution.py:176
  111.7 5.7 %fusion.47 = f32[8,1,4,2,32,64]{5,1,4,3,2,0:T(1,128)} fusion(pred[2,8,1,1,1,1]{0,2,5,4,3,1:T(4,128)(4,1)S(1)} %copy.268, f32[2,8,4,2,32,64]{5,1,4,0,2,3:T(8,128)S(1)} %fusion.49), kind=kOutput, calls=%fused_computation.69 | convolution fusion | flops 3145728 | bytes 1572880 | tf_op jit(solution)/shard_map/rj,rjugkp->jugkp/dot_general | solution.py:179
  117.5 7.9 %fusion = f32[2,32,256,64]{2,3,1,0:T(8,128)} fusion(bf16[256,2,32,64]{0,3,2,1:T(8,128)(2,1)} %bitcast.237, f32[2,32,256]{2,1,0:T(8,128)} %bitcast.263, f32[2,32,256]{2,1,0:T(8,128)S(1)} %copy-done.42, f32[2,256,256]{2,1,0:T(8,128)} %fusion.88, pred[256,256]{1,0:T(8,128)(4,1)S(1)} %copy-done.40), kind=kOutput, calls=%fused_computation.2 | convolution fusion | flops 562036736 | bytes 7012352 | tf_op jit(solution)/shard_map/gkts,sgkp->tgkp/dot_general | solution.py:34
  132.0 4.0 fusion.58
  137.3 6.5 %fusion.1 = f32[2,32,256,64]{2,3,1,0:T(8,128)} fusion(bf16[256,2,32,64]{0,3,2,1:T(8,128)(2,1)S(1)} %bitcast.240, f32[2,32,256]{2,1,0:T(8,128)S(1)} %bitcast.262, f32[2,32,256]{2,1,0:T(8,128)S(1)} %copy-done.43, f32[2,256,256]{2,1,0:T(8,128)S(1)} %copy-done.35, pred[256,256]{1,0:T(8,128)(4,1)S(1)} %copy-done.41), kind=kOutput, calls=%fused_computation.3 | convolution fusion | flops 562036736 | bytes 7012352 | tf_op jit(solution)/shard_map/gkts,sgkp->tgkp/dot_general | solution.py:34
  143.9 41.0 %collective-permute-done.1 = bf16[2,2,32,32,128]{4,3,2,1,0:T(8,128)(2,1)} collective-permute-done((bf16[2,2,32,32,128]{4,3,2,1,0:T(8,128)(2,1)}, bf16[2,2,32,32,128]{4,3,2,1,0:T(8,128)(2,1)}, u32[]{:S(2)}, u32[]{:S(2)}) %collective-permute-start.1) | collective-permute-done | bytes 1048608 | tf_op jit(solution)/shard_map/ppermute | solution.py:73
  184.9 2.9 fusion.30
  196.8 2.5 reshape_reshape.15
  202.1 2.6 broadcast_multiply_fusion
  204.7 87.2 %collective-permute-done.2 = bf16[2,2,32,32,128]{4,3,2,1,0:T(8,128)(2,1)} collective-permute-done((bf16[2,2,32,32,128]{4,3,2,1,0:T(8,128)(2,1)}, bf16[2,2,32,32,128]{4,3,2,1,0:T(8,128)(2,1)}, u32[]{:S(2)}, u32[]{:S(2)}) %collective-permute-start.2) | collective-permute-done | bytes 1048608 | tf_op jit(solution)/shard_map/ppermute | solution.py:73
  292.0 2.9 select_convert_fusion
  356.9 2.6 convert_select_fusion.1
  361.0 4.0 fusion.18
  365.0 4.3 %copy.225 = bf16[1,256,4096]{2,1,0:T(8,128)(2,1)} copy(bf16[1,256,4096]{1,2,0:T(8,128)(2,1)} %bitcast.243) | data formatting | bytes 4194304 | tf_op jit(solution)/shard_map/convert_element_type | solution.py:58
  369.3 6.6 %fusion.21 = bf16[256,2,32,64]{0,3,2,1:T(8,128)(2,1)} fusion(bf16[256,2,32,64]{0,3,2,1:T(8,128)(2,1)S(1)} %bitcast.241, f32[2,32,256,64]{2,3,1,0:T(8,128)} %fusion.1, bf16[256,2,128,1]{0,2,3,1:T(8,128)(2,1)S(1)} %bitcast.248, f32[2,2,32,32,128]{4,3,2,1,0:T(8,128)} %copy-done.7, f32[2,2,32,32,128]{4,3,2,1,0:T(8,128)} %copy-done.6, ...), kind=kOutput, calls=%fused_computation.32 | convolution fusion | flops 1617428480 | bytes 12779776 | tf_op jit(solution)/shard_map/tgn,gkpn->tgkp/dot_general | solution.py:51
  375.9 4.3 %copy.226 = bf16[1,256,4096]{2,1,0:T(8,128)(2,1)} copy(bf16[1,256,4096]{1,2,0:T(8,128)(2,1)} %bitcast.242) | data formatting | bytes 4194304 | tf_op jit(solution)/shard_map/convert_element_type | solution.py:58
  380.2 4.0 pad_maximum_fusion.1
  384.2 4.6 %reduce_sum.69 = f32[8,4,2,32,64]{4,3,2,1,0:T(8,128)S(1)} reduce(f32[8,8,4,2,32,64]{5,4,3,2,1,0:T(8,128)} %bitcast.244, f32[]{:T(128)} %constant.38.clone.1), dimensions={0}, to_apply=%region_11.12 | reduce | flops 917504 | bytes 4718596 | tf_op jit(solution)/shard_map/reduce_sum | solution.py:180
  392.2 4.9 %fusion.2 = f32[8,4,1024]{2,0,1:T(8,128)S(1)} fusion(bf16[4096,1024]{1,0:T(8,128)(2,1)} %param.25, bf16[8,1,4096]{2,0,1:T(8,128)(2,1)S(1)} %get-tuple-element.41, bf16[8,1,4096]{2,0,1:T(8,128)(2,1)S(1)} %get-tuple-element.40, bf16[8,1,4096]{2,0,1:T(8,128)(2,1)S(1)} %get-tuple-element.47, bf16[8,1,4096]{2,0,1:T(8,128)(2,1)S(1)} %get-tuple-element.46), kind=kOutput, calls=%fused_computation.4 | convolution fusion | flops 268828672 | bytes 8781824 | tf_op jit(solution)/shard_map/jup,pd->jud/dot_general | solution.py:194
  397.1 3.8 all-reduce.5
  (294 shorter events, 118.5 us)
Async XLA Ops:
  7.2 11.5 %copy-start.36 = (f32[2,64,256]{2,1,0:T(8,128)S(1)}, f32[2,64,256]{2,1,0:T(8,128)}, u32[]{:S(2)}) copy-start(f32[2,64,256]{2,1,0:T(8,128)} %param.16) | copy-start | bytes 393220
  7.2 85.4 %all-reduce.4.cloned.1.call-start = ((), (), s32[]{:S(2)}) async-start(), calls=%async_computation.1 | async-start | bytes 1228800
  9.0 14.4 %copy-start.51 = (f32[64,2]{0,1:T(2,128)}, f32[64,2]{0,1:T(2,128)S(1)}, u32[]{:S(2)}) copy-start(f32[64,2]{0,1:T(2,128)S(1)} %slice.199) | copy-start | bytes 1540
  18.6 365.6 %all-gather.4.cloned.1.call-start = ((), (), s32[]{:S(2)}) async-start(), calls=%async_computation | async-start | bytes 9437184 | tf_op jit(solution)/shard_map/all_gather | solution.py:180
  35.2 96.7 %collective-permute-start = (bf16[2,2,32,32,128]{4,3,2,1,0:T(8,128)(2,1)}, bf16[2,2,32,32,128]{4,3,2,1,0:T(8,128)(2,1)S(1)}, u32[]{:S(2)}, u32[]{:S(2)}) collective-permute-start(bf16[2,2,32,32,128]{4,3,2,1,0:T(8,128)(2,1)} %select_convert_fusion.1), channel_id=1, source_target_pairs={{0,2},{4,6},{8,10},{12,14},{2,0},{6,4},{10,8},{14,12},{1,3},{5,7},... | collective-permute-start | bytes 3145736 | tf_op jit(solution)/shard_map/ppermute | solution.py:73
  117.5 7.9 %copy-start.62 = (f32[64]{0:T(128)S(1)}, f32[64]{0:T(128)}, u32[]{:S(2)}) copy-start(f32[64]{0:T(128)} %param.18) | copy-start | bytes 772
  135.9 48.9 %collective-permute-start.1 = (bf16[2,2,32,32,128]{4,3,2,1,0:T(8,128)(2,1)}, bf16[2,2,32,32,128]{4,3,2,1,0:T(8,128)(2,1)}, u32[]{:S(2)}, u32[]{:S(2)}) collective-permute-start(bf16[2,2,32,32,128]{4,3,2,1,0:T(8,128)(2,1)} %get-tuple-element.18), channel_id=1, source_target_pairs={{0,4},{4,8},{8,12},{2,6},{6,10},{10,14},{1,5},{5,9},{9,13},{3,7},{... | collective-permute-start | bytes 3145736 | tf_op jit(solution)/shard_map/ppermute | solution.py:73
  137.3 6.5 %copy-start.61 = (f32[128]{0:T(128)S(1)}, f32[128]{0:T(128)}, u32[]{:S(2)}) copy-start(f32[128]{0:T(128)} %get-tuple-element.13) | copy-start | bytes 1540
  137.3 47.6 %copy-start.1 = (f32[2,2,32,32,128]{4,3,2,1,0:T(8,128)S(1)}, f32[2,2,32,32,128]{4,3,2,1,0:T(8,128)}, u32[]{:S(2)}) copy-start(f32[2,2,32,32,128]{4,3,2,1,0:T(8,128)} %get-tuple-element.19) | copy-start | bytes 6291460
  187.8 104.2 %collective-permute-start.2 = (bf16[2,2,32,32,128]{4,3,2,1,0:T(8,128)(2,1)}, bf16[2,2,32,32,128]{4,3,2,1,0:T(8,128)(2,1)}, u32[]{:S(2)}, u32[]{:S(2)}) collective-permute-start(bf16[2,2,32,32,128]{4,3,2,1,0:T(8,128)(2,1)} %fusion.30), channel_id=1, source_target_pairs={{0,8},{4,12},{2,10},{6,14},{1,9},{5,13},{3,11},{7,15},{16,24},{20,... | collective-permute-start | bytes 3145736 | tf_op jit(solution)/shard_map/ppermute | solution.py:73
  200.1 94.7 %copy-start.45 = (f32[2,2,32]{2,1,0:T(2,128)}, f32[2,2,32]{2,1,0:T(2,128)S(1)}, u32[]{:S(2)}) copy-start(f32[2,2,32]{2,1,0:T(2,128)S(1)} %exp.222) | copy-start | bytes 1540
  200.9 94.0 %copy-start.47 = (f32[2,2,32]{2,1,0:T(2,128)}, f32[2,2,32]{2,1,0:T(2,128)S(1)}, u32[]{:S(2)}) copy-start(f32[2,2,32]{2,1,0:T(2,128)S(1)} %exp.230) | copy-start | bytes 1540
  202.1 89.9 %copy-start.49 = (f32[2,2,32]{2,1,0:T(2,128)S(1)}, f32[2,2,32]{2,1,0:T(2,128)}, u32[]{:S(2)}) copy-start(f32[2,2,32]{2,1,0:T(2,128)} %exp.232) | copy-start | bytes 1540
  204.7 91.7 %copy-start.52 = (f32[8,2]{1,0:T(8,128)S(1)}, f32[8,2]{1,0:T(8,128)}, u32[]{:S(2)}) copy-start(f32[8,2]{1,0:T(8,128)} %copy.232) | copy-start | bytes 196
  204.7 91.7 %copy-start.53 = (f32[8,2]{1,0:T(8,128)S(1)}, f32[8,2]{1,0:T(8,128)}, u32[]{:S(2)}) copy-start(f32[8,2]{1,0:T(8,128)} %copy.237) | copy-start | bytes 196
  204.7 91.7 %copy-start.54 = (f32[8,2]{1,0:T(8,128)S(1)}, f32[8,2]{1,0:T(8,128)}, u32[]{:S(2)}) copy-start(f32[8,2]{1,0:T(8,128)} %copy.239) | copy-start | bytes 196
  204.7 91.7 %copy-start.55 = (f32[8,2]{1,0:T(8,128)S(1)}, f32[8,2]{1,0:T(8,128)}, u32[]{:S(2)}) copy-start(f32[8,2]{1,0:T(8,128)} %copy.242) | copy-start | bytes 196
  204.7 91.7 %copy-start.56 = (f32[8,2]{1,0:T(8,128)S(1)}, f32[8,2]{1,0:T(8,128)}, u32[]{:S(2)}) copy-start(f32[8,2]{1,0:T(8,128)} %copy.244) | copy-start | bytes 196
  204.7 91.7 %copy-start.57 = (f32[8,2]{1,0:T(8,128)S(1)}, f32[8,2]{1,0:T(8,128)}, u32[]{:S(2)}) copy-start(f32[8,2]{1,0:T(8,128)} %copy.246) | copy-start | bytes 196
  204.7 91.7 %copy-start.58 = (f32[8,2]{1,0:T(8,128)S(1)}, f32[8,2]{1,0:T(8,128)}, u32[]{:S(2)}) copy-start(f32[8,2]{1,0:T(8,128)} %copy.249) | copy-start | bytes 196
  294.9 62.0 %collective-permute-start.3 = (bf16[2,2,32,32,128]{4,3,2,1,0:T(8,128)(2,1)}, bf16[2,2,32,32,128]{4,3,2,1,0:T(8,128)(2,1)}, u32[]{:S(2)}, u32[]{:S(2)}) collective-permute-start(bf16[2,2,32,32,128]{4,3,2,1,0:T(8,128)(2,1)} %select_convert_fusion), channel_id=1, source_target_pairs={{0,2},{4,6},{8,10},{12,14},{2,0},{6,4},{10,8},{14,12},{1,3},{5,7},... | collective-permute-start | bytes 3145736 | tf_op jit(solution)/shard_map/ppermute | solution.py:73
  339.8 17.1 %copy-start.46 = (f32[2,2,32]{2,1,0:T(2,128)S(1)}, f32[2,2,32]{2,1,0:T(2,128)}, u32[]{:S(2)}) copy-start(f32[2,2,32]{2,1,0:T(2,128)} %copy-done.45) | copy-start | bytes 1540
  339.8 17.1 %copy-start.48 = (f32[2,2,32]{2,1,0:T(2,128)S(1)}, f32[2,2,32]{2,1,0:T(2,128)}, u32[]{:S(2)}) copy-start(f32[2,2,32]{2,1,0:T(2,128)} %copy-done.47) | copy-start | bytes 1540
  339.8 17.1 %copy-start.50 = (f32[2,2,32]{2,1,0:T(2,128)S(1)}, f32[2,2,32]{2,1,0:T(2,128)}, u32[]{:S(2)}) copy-start(f32[2,2,32]{2,1,0:T(2,128)} %exp.232) | copy-start | bytes 1540
  (45 other events, 145.8 us)
Sparse Core Ops, SparseCore 0:
  18.7 73.7 all-reduce.3
  117.6 185.2 all-gather.3
